TPU v7x, 128 devices: a whole 4x4x4 slice. The times are simulated.
128 devices in a mesh: gz: 64 (over x, y_lo, z, core), xy: 2 (over y_hi).
Axes of the slice: x: 4, y: 4 (y_hi: 2, y_lo: 2; y = y_hi * 2 + y_lo), z: 4, core: 2. Of those that a mesh axis runs over, the one named last changes fastest.
Arguments:
- moments: bfloat16 [361, 512, 256], P(None, 'gz', 'xy'), may hold values from -4 to 4
- counts: int32 [512, 256], P('gz', 'xy'), may hold values from 0 to 7
- m2x: bfloat16 [1296, 361], replicated, may hold values from -0.3125 to 0.3125
- x2l: bfloat16 [361, 1296], replicated, may hold values from -0.0625 to 0.0625
- decay_rate: float32 [648], replicated, may hold values from 0.00048828125 to 0.05
- wave_x: float32 [648], replicated, may hold values from -3.140625 to 3.140625
- wave_y: float32 [648], replicated, may hold values from -3.140625 to 3.140625
- offsets: int32 [6, 2], replicated, may hold values from -2 to 2, as said below
Outputs:
- local_out: bfloat16 [361, 512, 256], P(None, 'gz', 'xy')
Inputs may be any that keep to these rules, and one draw needn't show every extreme that they name: `offsets`: some row is (2, -2) and some row is (-2, 2).
All inputs are finite; a program needn't handle non-finite values.
Results may differ from a plain program's by a relative error of at most 0.0064.
Values may be sent and summed in bfloat16 or wider, within the bound.
No kernel may reach another device: no remote copies, remote signals or barrier semaphores. Data moves between devices by JAX's collectives and lax.ppermute only.
A program may use at most 192 MiB of HBM per device.

v0:
```python
import jax
import jax.numpy as jnp
from jax import lax
from jax.sharding import PartitionSpec as P

BY = 8
R = 2
NOFF = 6


def from_behind(value, axis, steps):
    count = lax.axis_size(axis)
    pairs = [(source, (source + steps) % count) for source in range(count)]
    return lax.ppermute(value, axis, pairs)


def entering_2(part, axis, combine, identity):
    place = lax.axis_index(axis)
    gathered = jax.tree.map(lambda a: lax.all_gather(a, axis), part)
    state = jax.tree.map(lambda a, e: jnp.zeros_like(a) + jnp.asarray(e, a.dtype), part, identity)

    def one(turn, state):
        return combine(
            state, jax.tree.map(lambda a: lax.dynamic_index_in_dim(a, turn, 0, False), gathered)
        )

    return lax.fori_loop(0, place, one, state)


def extended(block, sides, width):
    for axis, dim in sides:
        count = lax.axis_size(axis)
        forward = [(i, i + 1) for i in range(count - 1)]
        forward.append((count - 1, 0))
        backward = [(target, source) for source, target in forward]
        low = lax.ppermute(
            lax.slice_in_dim(block, block.shape[dim] - width, None, axis=dim), axis, forward
        )
        high = lax.ppermute(lax.slice_in_dim(block, 0, width, axis=dim), axis, backward)
        block = jnp.concatenate([low, block, high], axis=dim)
    return block


def build_upward(box_terms, entering, before_term, rate_col, factor):
    layers = box_terms.shape[1]
    layer_pos = jnp.arange(layers, dtype=jnp.float32)
    layer_gap = layer_pos[:, None] - layer_pos[None, :]
    decay_table = jnp.where(
        layer_gap[None] >= 2.0,
        jnp.exp(-rate_col[:, :, None] * jnp.maximum(layer_gap, 0.0)[None]),
        0.0,
    )
    upward = jnp.einsum("kij,kjb->kib", decay_table, box_terms, precision=lax.Precision.HIGHEST)
    upward = (
        upward + jnp.exp(-rate_col * (layer_pos + 1.0)[None, :])[:, :, None] * entering[:, None, :]
    )
    upward = upward.at[:, 0, :].add(-factor * before_term)
    return upward


def body(moments, counts, m2x, x2l, decay_rate, wave_x, wave_y, offsets):
    coeffs, layers, plane_size = moments.shape
    exp_rows = m2x.shape[0]
    half_rows = exp_rows // 2
    columns = plane_size // BY
    loop_size = lax.axis_size("gz")
    slab_pos = lax.axis_index("gz").astype(jnp.float32)
    rate_col = jnp.concatenate([decay_rate, decay_rate])[:, None]
    factor = jnp.exp(-rate_col)
    weight = jnp.sqrt(1.0 - factor * factor)
    multipole = (moments.astype(jnp.float32) * counts.astype(jnp.float32)[None]).astype(
        jnp.bfloat16
    )
    expansion = jnp.dot(
        m2x, multipole.reshape(coeffs, layers * plane_size), preferred_element_type=jnp.float32
    )
    box_terms = (weight * expansion).reshape(exp_rows, layers, plane_size)
    layer_pos = jnp.arange(layers, dtype=jnp.float32)
    tail_power = jnp.exp(-rate_col * (layers - 1.0 - layer_pos)[None, :])
    outgoing = jnp.einsum("kz,kzb->kb", tail_power, box_terms, precision=lax.Precision.HIGHEST)
    before_term = from_behind(box_terms[:, layers - 1, :].astype(jnp.bfloat16), "gz", 1).astype(
        jnp.float32
    )
    slab_decay = jnp.exp(-rate_col * layers)
    lap_gain = 1.0 - jnp.exp(-rate_col * (layers * loop_size))

    def combine(earlier, later):
        return (earlier[0] * later[0], later[0] * earlier[1] + later[1])

    identity = (jnp.ones_like(slab_decay), jnp.zeros_like(outgoing))
    _, prefix = entering_2((slab_decay, outgoing), "gz", combine, identity)
    scaled = jnp.exp(-rate_col * (layers * (loop_size - 1.0 - slab_pos))) * outgoing
    lap_sum = lax.psum(scaled, "gz")
    entering = prefix + jnp.exp(-rate_col * (layers * slab_pos)) * lap_sum / lap_gain
    upward = build_upward(box_terms, entering, before_term, rate_col, factor)
    field_grid = upward.astype(jnp.bfloat16).reshape(exp_rows, layers, columns, BY)
    padded = extended(field_grid, (("xy", 2),), R)
    acc_real = jnp.zeros((half_rows, layers, columns, BY), jnp.float32)
    acc_imag = jnp.zeros((half_rows, layers, columns, BY), jnp.float32)
    for list_entry in range(NOFF):
        step_x = offsets[list_entry, 0]
        step_y = offsets[list_entry, 1]
        moved = lax.dynamic_slice_in_dim(padded, R - step_x, columns, 2)
        moved = jnp.roll(moved, step_y, axis=3)
        phase_angle = wave_x * step_x.astype(jnp.float32) + wave_y * step_y.astype(jnp.float32)
        cosine = jnp.cos(phase_angle)[:, None, None, None]
        sine_part = jnp.sin(phase_angle)[:, None, None, None]
        part_real = moved[:half_rows].astype(jnp.float32)
        part_imag = moved[half_rows:].astype(jnp.float32)
        acc_real = acc_real + part_real * cosine - part_imag * sine_part
        acc_imag = acc_imag + part_real * sine_part + part_imag * cosine
    shifted = (
        jnp.concatenate([acc_real, acc_imag], axis=0)
        .astype(jnp.bfloat16)
        .reshape(exp_rows, layers * plane_size)
    )
    local_out = jnp.dot(x2l, shifted, preferred_element_type=jnp.float32).astype(jnp.bfloat16)
    return local_out.reshape(coeffs, layers, plane_size)


def solution(mesh):
    in_specs = (P(None, "gz", "xy"), P("gz", "xy"), P(), P(), P(), P(), P(), P())
    out_specs = P(None, "gz", "xy")
    return jax.shard_map(body, mesh=mesh, in_specs=in_specs, out_specs=out_specs, check_vma=False)
```

profile of v0, /device:TPU:0, one launch (start us, length us, event | category | flops | bytes accessed | tf_op | source)
XLA Modules:
  0.0 901.1 jit_solution(17682668748722414921)
XLA Ops:
  10.6 1.6 multiply_bitcast_fusion
  13.5 9.6 %fusion.68 = f32[1296,1,128]{2,1,0:T(1,128)} fusion(f32[1296,8,1]{1,2,0:T(1,128)S(1)} %copy.17, f32[1296,8,128]{2,1,0:T(8,128)S(1)} %bitcast.59), kind=kOutput, calls=%fused_computation.135 | convolution fusion | flops 15925248 | bytes 6013440 | tf_op jit(solution)/shard_map/kz,kzb->kb/dot_general | solution.py:80
  23.1 2.9 slice.133
  27.7 85.2 %all_gather.10 = f32[64,1296,1]{1,2,0:T(1,128)S(1)} all-gather(f32[1,1296,1]{1,2,0:T(1,128)S(1)} %fusion.49), channel_id=1, replica_groups=mesh['gz'=64,'xy'=2] {'gz'}, dimensions={0}, use_global_device_ids=true | all-gather | bytes 336960 | tf_op jit(solution)/shard_map/all_gather | solution.py:19
  113.2 147.7 %all-gather.3.cloned.1.call-done = f32[82944,128]{1,0:T(8,128)} async-done(((f32[1296,128]{1,0:T(8,128)}), f32[82944,128]{1,0:T(8,128)}) %all-gather.3.cloned.1.call-update) | async-done | bytes 42467344 | tf_op jit(solution)/shard_map/all_gather | solution.py:19
  261.2 518.6 %all-reduce.2.cloned.1.call-done = f32[1296,128]{1,0:T(8,128)} async-done(((f32[1296,128]{1,0:T(8,128)}), f32[1296,128]{1,0:T(8,128)}) %all-reduce.2.cloned.1.call-update) | async-done | bytes 663568 | tf_op jit(solution)/shard_map/psum | solution.py:93
  779.7 1.5 divide_add_fusion
  781.2 13.8 %multiply_add_fusion = f32[1296,8,128]{2,1,0:T(8,128)S(1)} fusion(f32[1296,128]{1,0:T(8,128)S(1)} %divide_add_fusion, f32[1296,8]{1,0:T(8,128)S(1)} %copy.14, f32[1296,8,128]{2,1,0:T(8,128)} %bitcast.61, f32[8,8]{1,0:T(8,128)S(1)} %fusion.50, f32[1296]{0:T(1024)S(1)} %get-tuple-element.100, pred[8,8]{1,0:T(8,128)(4,1)S(1)} %fusion.51), kind=kOutput, calls=%fused_computation.14 | convolution fusion | flops 130222080 | bytes 11327360 | tf_op jit(solution)/shard_map/kij,kjb->kib/dot_general | solution.py:53
  795.1 2.4 copy-done.3
  798.2 18.9 %scatter-add.4 = f32[1296,8,128]{2,1,0:T(8,128)} dynamic-update-slice(f32[1296,8,128]{2,1,0:T(8,128)} %copy-done.3, f32[1296,1,128]{2,1,0:T(1,128)S(1)} %slice_add_fusion, s32[]{:T(128)} %constant.97.clone.1, s32[]{:T(128)} %constant.97.clone.1, s32[]{:T(128)} %constant.97.clone.1) | dynamic-update-slice | bytes 1327108 | tf_op jit(solution)/shard_map/scatter-add | solution.py:57
  817.1 3.8 convert_element_type.126
  820.8 4.9 copy.16
  826.9 3.2 collective-permute-start.1
  856.9 2.1 pad_maximum_fusion
  859.0 3.4 constant_dynamic-slice_fusion.5
  862.4 4.7 fusion.29
  867.1 2.0 fusion.30
  869.1 2.0 fusion.31
  871.2 2.1 fusion.32
  873.3 2.1 fusion.33
  875.3 2.3 fusion.28
  877.6 7.1 fusion.15
  884.7 6.9 fusion.27
  891.7 1.5 fusion.44
  (53 shorter events, 11.6 us)
Async XLA Ops:
  6.5 4.0 copy-start
  6.5 254.4 %all-gather.3.cloned.1.call-start = ((), (), s32[]{:S(2)}) async-start(), calls=%async_computation.1 | async-start | bytes 43130880 | tf_op jit(solution)/shard_map/all_gather | solution.py:19
  13.5 9.6 %copy-start.2 = (f32[162,8,8,128]{3,2,1,0:T(8,128)}, f32[162,8,8,128]{3,2,1,0:T(8,128)S(1)}, u32[]{:S(2)}) copy-start(f32[162,8,8,128]{3,2,1,0:T(8,128)S(1)} %copy.22) | copy-start | bytes 15925252
  23.1 3.1 copy-start.4
  23.1 4.3 copy-start.6
  23.1 756.7 %all-reduce.2.cloned.1.call-start = ((), (), s32[]{:S(2)}) async-start(), calls=%async_computation | async-start | bytes 1327104 | tf_op jit(solution)/shard_map/psum | solution.py:93
  26.1 86.8 %collective-permute-start = (bf16[1296,128]{1,0:T(8,128)(2,1)S(1)}, bf16[1296,128]{1,0:T(8,128)(2,1)S(1)}, u32[]{:S(2)}, u32[]{:S(2)}) collective-permute-start(bf16[1296,128]{1,0:T(8,128)(2,1)S(1)} %bitcast.73), channel_id=1, source_target_pairs={{0,2},{2,4},{4,6},{6,8},{8,10},{10,12},{12,14},{14,16},{16,18},{18... | collective-permute-start | bytes 995336 | tf_op jit(solution)/shard_map/ppermute | solution.py:14
  795.1 2.4 copy-start.3
  820.8 9.6 %copy-start.5 = (s32[6,2]{0,1:T(2,128)S(1)}, s32[6,2]{0,1:T(2,128)}, u32[]{:S(2)}) copy-start(s32[6,2]{0,1:T(2,128)} %param.21) | copy-start | bytes 148
  820.8 35.9 %copy-start.7 = (f32[648]{0:T(1024)S(1)}, f32[648]{0:T(1024)}, u32[]{:S(2)}) copy-start(f32[648]{0:T(1024)} %param.20) | copy-start | bytes 7780
  820.8 35.9 %copy-start.8 = (f32[648]{0:T(1024)S(1)}, f32[648]{0:T(1024)}, u32[]{:S(2)}) copy-start(f32[648]{0:T(1024)} %param.19) | copy-start | bytes 7780
  826.9 30.0 %collective-permute-start.1 = (bf16[1296,8,2,8]{0,3,2,1:T(8,128)(2,1)S(1)}, bf16[1296,8,2,8]{0,3,2,1:T(8,128)(2,1)S(1)}, u32[]{:S(2)}, u32[]{:S(2)}) collective-permute-start(bf16[1296,8,2,8]{0,3,2,1:T(8,128)(2,1)S(1)} %get-tuple-element.79), channel_id=1, source_target_pairs={{0,1},{1,0},{2,3},{3,2},{4,5},{5,4},{6,7},{7,6},{8,9},{9,8},{10,11... | collective-permute-start | bytes 995336 | tf_op jit(solution)/shard_map/ppermute | solution.py:36
  830.1 26.9 %collective-permute-start.2 = (bf16[1296,8,2,8]{0,3,2,1:T(8,128)(2,1)S(1)}, bf16[1296,8,2,8]{0,3,2,1:T(8,128)(2,1)S(1)}, u32[]{:S(2)}, u32[]{:S(2)}) collective-permute-start(bf16[1296,8,2,8]{0,3,2,1:T(8,128)(2,1)S(1)} %get-tuple-element.80), channel_id=1, source_target_pairs={{1,0},{0,1},{3,2},{2,3},{5,4},{4,5},{7,6},{6,7},{9,8},{8,9},{11,10... | collective-permute-start | bytes 995336 | tf_op jit(solution)/shard_map/ppermute | solution.py:39
  884.7 7.0 copy-start.9
  891.7 2.6 copy-start.1
Sparse Core Ops, SparseCore 0:
  23.2 237.6 all-gather.2
  263.4 516.2 all-reduce.1
where the time goes:
time: 905 us; the launch traced here: 901 us
  waiting for transfers between devices  666 us (74%)
  blocking collectives  85.2 us (9%)
  other arithmetic  41.8 us (5%)
  between operations  39.3 us (4%)
  local copies, waits for them, and re-layouts  38 us (4%)
  matrix products  26.5 us (3%)
    psum x1, waiting for transfers between devices, body(): lap_sum = lax.psum(scaled, 'gz')  519 us
    all_gather x1, waiting for transfers between devices, entering_2(): gathered = jax.tree.map(lambda a: lax.all_gather(a, axis), part)  148 us
    all_gather x1, blocking collectives, entering_2(): gathered = jax.tree.map(lambda a: lax.all_gather(a, axis), part)  85.2 us
    scatter-add x1, local copies, waits for them, and re-layouts, build_upward(): upward = upward.at[:, 0, :].add(-factor * before_term)  18.9 us
  transfers between devices with their start and end apart: 5, of which 2 were waited for; matrix products, arithmetic and copies ran while one was open for 1% of the time, Pallas kernels for 0%

commit v1 on v0

--- a/solution.py
+++ b/solution.py
@@ -6,6 +6,10 @@
 BY = 8
 R = 2
 NOFF = 6
+
+
+def blocks_answer(u_in):
+    return jnp.sum(lax.all_gather(u_in, "gz"), axis=0)
 
 
 def from_behind(value, axis, steps):
@@ -90,7 +94,7 @@
     identity = (jnp.ones_like(slab_decay), jnp.zeros_like(outgoing))
     _, prefix = entering_2((slab_decay, outgoing), "gz", combine, identity)
     scaled = jnp.exp(-rate_col * (layers * (loop_size - 1.0 - slab_pos))) * outgoing
-    lap_sum = lax.psum(scaled, "gz")
+    lap_sum = blocks_answer(scaled)
     entering = prefix + jnp.exp(-rate_col * (layers * slab_pos)) * lap_sum / lap_gain
     upward = build_upward(box_terms, entering, before_term, rate_col, factor)
     field_grid = upward.astype(jnp.bfloat16).reshape(exp_rows, layers, columns, BY)

time: 905 us -> 710 us (0.78)
  the two profiles are of different devices: /device:TPU:0 before, /device:TPU:111 now
where the time goes in v1:
time: 710 us; the launch traced here: 706 us
  waiting for transfers between devices  375 us (53%)
  other arithmetic  143 us (20%)
  blocking collectives  77.7 us (11%)
  local copies, waits for them, and re-layouts  39.6 us (6%)
  between operations  39.3 us (6%)
  matrix products  25.7 us (4%)
    all_gather x1, waiting for transfers between devices, entering_2(): gathered = jax.tree.map(lambda a: lax.all_gather(a, axis), part)  220 us
    all_gather x1, waiting for transfers between devices, blocks_answer(): return jnp.sum(lax.all_gather(u_in, 'gz'), axis=0)  154 us
    add x63, other arithmetic, combine(): return (earlier[0] * later[0], later[0] * earlier[1] + later[1])  86.8 us
    all_gather x1, blocking collectives, entering_2(): gathered = jax.tree.map(lambda a: lax.all_gather(a, axis), part)  77.7 us
    scatter-add x1, local copies, waits for them, and re-layouts, build_upward(): upward = upward.at[:, 0, :].add(-factor * before_term)  18.9 us
    reduce_sum x1, other arithmetic, blocks_answer(): return jnp.sum(lax.all_gather(u_in, 'gz'), axis=0)  15.7 us
    concatenate x6, other arithmetic, body(): moved = jnp.roll(moved, step_y, axis=3)  15.2 us
  transfers between devices with their start and end apart: 5, of which 2 were waited for; matrix products, arithmetic and copies ran while one was open for 3% of the time, Pallas kernels for 0%

profile of v1, /device:TPU:111, one launch (start us, length us, event | category | flops | bytes accessed | tf_op | source)
XLA Modules:
  0.0 706.3 jit_solution(16840397034992762555)
XLA Ops:
  10.6 1.6 multiply_bitcast_fusion
  13.5 8.9 %fusion.68 = f32[1296,1,128]{2,1,0:T(1,128)S(1)} fusion(f32[1296,8,1]{1,2,0:T(1,128)S(1)} %copy.17, f32[1296,8,128]{2,1,0:T(8,128)S(1)} %bitcast.61), kind=kOutput, calls=%fused_computation.135 | convolution fusion | flops 15925248 | bytes 6013440 | tf_op jit(solution)/shard_map/kz,kzb->kb/dot_general | solution.py:84
  24.2 2.9 slice.133
  27.6 77.7 %all_gather.16 = f32[64,1296,1]{1,2,0:T(1,128)S(1)} all-gather(f32[1,1296,1]{1,2,0:T(1,128)S(1)} %fusion.49), channel_id=1, replica_groups=mesh['gz'=64,'xy'=2] {'gz'}, dimensions={0}, use_global_device_ids=true | all-gather | bytes 336960 | tf_op jit(solution)/shard_map/all_gather | solution.py:23
  105.5 154.3 %all-gather.7.cloned.1.call-done = f32[82944,128]{1,0:T(8,128)} async-done(((f32[1296,128]{1,0:T(8,128)}), f32[82944,128]{1,0:T(8,128)}) %all-gather.7.cloned.1.call-update) | async-done | bytes 42467344 | tf_op jit(solution)/shard_map/all_gather | solution.py:12
  259.8 15.7 %reduce_sum.9 = f32[1296,128]{1,0:T(8,128)S(1)} reduce(f32[64,1296,128]{2,1,0:T(8,128)} %bitcast.60, f32[]{:T(128)} %constant.95.clone.1), dimensions={0}, to_apply=%region_2.3 | reduce | flops 10450944 | bytes 43130884 | tf_op jit(solution)/shard_map/reduce_sum | solution.py:12
  275.5 220.0 %all-gather.5.cloned.1.call-done = f32[82944,128]{1,0:T(8,128)} async-done(((f32[1296,128]{1,0:T(8,128)}), f32[82944,128]{1,0:T(8,128)}) %all-gather.5.cloned.1.call-update) | async-done | bytes 42467344 | tf_op jit(solution)/shard_map/all_gather | solution.py:23
  495.6 91.1 %while.13 = (s32[]{:T(128)}, f32[1296,128]{1,0:T(8,128)S(1)}, s32[]{:T(128)}, f32[64,1296,1]{1,2,0:T(1,128)S(1)}, f32[64,1296,128]{2,1,0:T(8,128)}, /*index=5*/s32[]{:T(128)}, s32[]{:T(128)}, s32[]{:T(128)}) while((s32[]{:T(128)}, f32[1296,128]{1,0:T(8,128)S(1)}, s32[]{:T(128)}, f32[64,1296,1]{1,2,0:T(1,128)S(1)}, f32[64,1296,128]{2,1,0:T(8,128)}, ...), condition=%wide.region_1.2_spmd, body=%wide.region_0.1_spmd.sunk | while | flops 331781 | bytes 2006335 | solution.py:31
  587.1 13.8 %multiply_add_fusion = f32[1296,8,128]{2,1,0:T(8,128)S(1)} fusion(f32[1296,128]{1,0:T(8,128)S(1)} %divide_add_fusion, f32[1296,8]{1,0:T(8,128)S(1)} %copy.14, f32[1296,8,128]{2,1,0:T(8,128)} %bitcast.63, f32[8,8]{1,0:T(8,128)S(1)} %fusion.50, f32[1296]{0:T(1024)S(1)} %get-tuple-element.100, pred[8,8]{1,0:T(8,128)(4,1)S(1)} %fusion.51), kind=kOutput, calls=%fused_computation.14 | convolution fusion | flops 130222080 | bytes 11327360 | tf_op jit(solution)/shard_map/kij,kjb->kib/dot_general | solution.py:57
  600.9 2.4 copy-done.3
  603.9 18.9 %scatter-add.4 = f32[1296,8,128]{2,1,0:T(8,128)} dynamic-update-slice(f32[1296,8,128]{2,1,0:T(8,128)} %copy-done.3, f32[1296,1,128]{2,1,0:T(1,128)S(1)} %slice_add_fusion, s32[]{:T(128)} %constant.97.clone.1, s32[]{:T(128)} %constant.97.clone.1, s32[]{:T(128)} %constant.97.clone.1) | dynamic-update-slice | bytes 1327108 | tf_op jit(solution)/shard_map/scatter-add | solution.py:61
  622.8 3.8 convert_element_type.126
  626.6 4.9 copy.16
  632.6 1.9 collective-permute-start.1
  662.1 2.1 pad_maximum_fusion
  664.2 3.4 constant_dynamic-slice_fusion.5
  667.6 4.7 fusion.29
  672.3 2.0 fusion.30
  674.3 2.0 fusion.31
  676.4 2.1 fusion.32
  678.4 2.1 fusion.33
  680.5 2.3 fusion.28
  682.8 7.1 %fusion.15 = bf16[648,8,16,8]{0,3,2,1:T(8,128)(2,1)S(1)} fusion(f32[648]{0:T(1024)S(1)} %get-tuple-element.84, f32[648]{0:T(1024)S(1)} %get-tuple-element.93, f32[648]{0:T(1024)S(1)} %get-tuple-element.85, f32[648]{0:T(1024)S(1)} %get-tuple-element.94, f32[648]{0:T(1024)S(1)} %get-tuple-element.86, f32[648]{0:T(1024)S(1)} %get-tuple-element.90, ...), kind=kLoop, calls=%fused_computation.56 | loop fusion | flops 23887872 | bytes 17283456 | tf_op jit(solution)/shard_map/convert.3
  689.9 6.9 fusion.27
  (180 shorter events, 103.1 us)
Async XLA Ops:
  6.5 4.0 copy-start
  6.5 253.3 %all-gather.7.cloned.1.call-start = ((), (), s32[]{:S(2)}) async-start(), calls=%async_computation.1 | async-start | bytes 43130880 | tf_op jit(solution)/shard_map/all_gather | solution.py:12
  13.5 8.9 %copy-start.2 = (f32[162,8,8,128]{3,2,1,0:T(8,128)}, f32[162,8,8,128]{3,2,1,0:T(8,128)S(1)}, u32[]{:S(2)}) copy-start(f32[162,8,8,128]{3,2,1,0:T(8,128)S(1)} %copy.22) | copy-start | bytes 15925252
  22.3 1.2 copy-start.4
  22.4 4.9 copy-start.6
  23.5 472.1 %all-gather.5.cloned.1.call-start = ((), (), s32[]{:S(2)}) async-start(), calls=%async_computation | async-start | bytes 43130880 | tf_op jit(solution)/shard_map/all_gather | solution.py:23
  27.2 78.1 %collective-permute-start = (bf16[1296,128]{1,0:T(8,128)(2,1)S(1)}, bf16[1296,128]{1,0:T(8,128)(2,1)S(1)}, u32[]{:S(2)}, u32[]{:S(2)}) collective-permute-start(bf16[1296,128]{1,0:T(8,128)(2,1)S(1)} %bitcast.75), channel_id=1, source_target_pairs={{0,2},{2,4},{4,6},{6,8},{8,10},{10,12},{12,14},{14,16},{16,18},{18... | collective-permute-start | bytes 995336 | tf_op jit(solution)/shard_map/ppermute | solution.py:18
  600.9 2.4 copy-start.3
  626.6 9.1 %copy-start.5 = (s32[6,2]{0,1:T(2,128)S(1)}, s32[6,2]{0,1:T(2,128)}, u32[]{:S(2)}) copy-start(s32[6,2]{0,1:T(2,128)} %param.21) | copy-start | bytes 148
  626.6 35.4 %copy-start.7 = (f32[648]{0:T(1024)S(1)}, f32[648]{0:T(1024)}, u32[]{:S(2)}) copy-start(f32[648]{0:T(1024)} %param.20) | copy-start | bytes 7780
  626.6 35.4 %copy-start.8 = (f32[648]{0:T(1024)S(1)}, f32[648]{0:T(1024)}, u32[]{:S(2)}) copy-start(f32[648]{0:T(1024)} %param.19) | copy-start | bytes 7780
  632.6 29.5 %collective-permute-start.1 = (bf16[1296,8,2,8]{0,3,2,1:T(8,128)(2,1)S(1)}, bf16[1296,8,2,8]{0,3,2,1:T(8,128)(2,1)S(1)}, u32[]{:S(2)}, u32[]{:S(2)}) collective-permute-start(bf16[1296,8,2,8]{0,3,2,1:T(8,128)(2,1)S(1)} %get-tuple-element.79), channel_id=1, source_target_pairs={{0,1},{1,0},{2,3},{3,2},{4,5},{5,4},{6,7},{7,6},{8,9},{9,8},{10,11... | collective-permute-start | bytes 995336 | tf_op jit(solution)/shard_map/ppermute | solution.py:40
  634.5 27.6 %collective-permute-start.2 = (bf16[1296,8,2,8]{0,3,2,1:T(8,128)(2,1)S(1)}, bf16[1296,8,2,8]{0,3,2,1:T(8,128)(2,1)S(1)}, u32[]{:S(2)}, u32[]{:S(2)}) collective-permute-start(bf16[1296,8,2,8]{0,3,2,1:T(8,128)(2,1)S(1)} %get-tuple-element.80), channel_id=1, source_target_pairs={{1,0},{0,1},{3,2},{2,3},{5,4},{4,5},{7,6},{6,7},{9,8},{8,9},{11,10... | collective-permute-start | bytes 995336 | tf_op jit(solution)/shard_map/ppermute | solution.py:43
  689.9 7.0 copy-start.9
  696.8 2.6 copy-start.1
Sparse Core Ops, SparseCore 0:
  23.6 236.1 all-gather.6
  261.6 233.9 all-gather.4
